TPU v7x, 32 devices: a whole 2x2x4 slice. The times are simulated.
32 devices in a mesh: groups: 2 (over y), slide: 4 (over z), rep: 2 (over x), section: 2 (over core).
Axes of the slice: x: 2, y: 2, z: 4, core: 2. Of those that a mesh axis runs over, the one named last changes fastest.
Arguments:
- tile_features: bfloat16 [8, 12, 49, 1536], P(('groups', 'rep', 'section'), 'slide'), parts along dimension 0, may hold values from -6 to 6
- depth_weight: float32 [49, 1536], replicated, may hold values from -0.875 to 0.875
- depth_bias: float32 [1536], replicated, may hold values from -3 to 3
- norm_gain: float32 [1536], replicated, may hold values from 0.1 to 1.9
- norm_bias: float32 [1536], replicated, may hold values from -3 to 3
- up_weight: bfloat16 [1536, 3072], P(None, 'rep'), may hold values from -0.15625 to 0.15625
- up_bias: float32 [3072], P('rep'), may hold values from -3 to 3
- down_weight: bfloat16 [3072, 1536], P('rep'), may hold values from -0.109375 to 0.109375
- down_bias: float32 [1536], replicated, may hold values from -3 to 3
- layer_scale: float32 [1536], replicated, may hold values from 0.3 to 3
- head_gain: float32 [1536], replicated, may hold values from 0.1 to 1.9
- head_bias: float32 [1536], replicated, may hold values from -3 to 3
- embed_store: bfloat16 [8, 512, 1536], P(('groups', 'rep', 'section'), 'slide'), parts along dimension 0, may hold values from -6 to 6
- in_weight: bfloat16 [1536, 1024], P('slide'), may hold values from -0.15625 to 0.15625
- slide_gain: float32 [1024], replicated, may hold values from 0.1 to 1.9
- qkv_weight: bfloat16 [1024, 3072], P(None, 'slide'), may hold values from -0.1875 to 0.1875
- head_slopes: float32 [16], replicated, may hold values from 0.004 to 0.4
- tile_coords: int32 [8, 2, 512], P(('groups', 'rep', 'section')), parts along dimension 0, may hold values from 0 to 95, as said below
- valid_counts: int32 [8], P(('groups', 'rep', 'section')), parts along dimension 0, may hold values from 128 to 512, as said below
Outputs:
- fresh_embed: bfloat16 [8, 12, 1536], P(('groups', 'rep', 'section'), 'slide'), parts along dimension 0
- context: bfloat16 [8, 512, 1024], P(('groups', 'rep', 'section'), 'slide'), parts along dimension 0
There are 2 independent parts, one for each index of `groups`. A program takes and returns all parts, laid end to end along the dimension named above; an argument that names none is the same for every part. Nothing has to cross between parts.
Inputs may be any that keep to these rules, and one draw needn't show every extreme that they name: `tile_coords`: each slide's 512 positions sit on distinct cells of a 96 by 96 grid, in raster order (by y, then x); the cells (0, 0) and (95, 95) are always among them. `valid_counts`: positions at or beyond a slide's count are padding.
All inputs are finite; a program needn't handle non-finite values.
Results may differ from a plain program's by a relative error of at most 0.0078.
Values may be sent and summed in bfloat16 or wider, within the bound.
No kernel may reach another device: no remote copies, remote signals or barrier semaphores. Data moves between devices by JAX's collectives and lax.ppermute only.
A program may use at most 64 MiB of HBM per device.

v0:
```python
import math
import jax
import jax.numpy as jnp
from jax import lax
from jax.sharding import PartitionSpec as P

SIDE = 7
KER = 7
HDIM = 64


def layer_norm(inputs, gain, shift, epsilon):
    center = jnp.mean(inputs, axis=-1, keepdims=True)
    centered = inputs - center
    spread = jnp.mean(centered * centered, axis=-1, keepdims=True)
    return centered * lax.rsqrt(spread + epsilon) * gain + shift


def depthwise(tile_data, depth_weight, depth_bias):
    tile_count = tile_data.shape[0]
    channels = tile_data.shape[-1]
    spatial = tile_data.reshape(tile_count, SIDE, SIDE, channels)
    margin = KER // 2
    padded = jnp.pad(spatial, ((0, 0), (margin, margin), (margin, margin), (0, 0)))
    running = jnp.zeros_like(spatial) + depth_bias
    for tap_row in range(KER):
        for tap_col in range(KER):
            running = (
                running
                + padded[:, tap_row : tap_row + SIDE, tap_col : tap_col + SIDE, :]
                * depth_weight[tap_row * KER + tap_col]
            )
    return running.reshape(tile_count, SIDE * SIDE, channels)


def normalize_heads(values):
    row_total = values.shape[0]
    grouped = values.reshape(row_total, -1, 3, HDIM)
    paired = grouped[:, :, :2]
    scaled = paired * lax.rsqrt(jnp.mean(paired * paired, axis=-1, keepdims=True) + 1e-06)
    joined = jnp.concatenate([scaled, grouped[:, :, 2:]], axis=2)
    return joined.astype(jnp.bfloat16).reshape(row_total, -1)


def on_device(
    tile_features,
    depth_weight,
    depth_bias,
    norm_gain,
    norm_bias,
    up_weight,
    up_bias,
    down_weight,
    down_bias,
    layer_scale,
    head_gain,
    head_bias,
    embed_store,
    in_weight,
    slide_gain,
    qkv_weight,
    head_slopes,
    tile_coords,
    valid_counts,
):
    tile_data = tile_features[0].astype(jnp.float32)
    fresh_count = tile_data.shape[0]
    channels = tile_data.shape[-1]
    convolved = depthwise(tile_data, depth_weight, depth_bias)
    normed = (
        layer_norm(convolved, norm_gain, norm_bias, 1e-06)
        .astype(jnp.bfloat16)
        .reshape(-1, channels)
    )
    hidden = jax.nn.gelu(
        jnp.dot(
            lax.all_gather(normed, "rep", axis=0, tiled=True),
            up_weight,
            preferred_element_type=jnp.float32,
        )
        + up_bias,
        approximate=False,
    ).astype(jnp.bfloat16)
    summed = lax.psum_scatter(
        jnp.dot(hidden, down_weight, preferred_element_type=jnp.float32).astype(jnp.bfloat16),
        "rep",
        scatter_dimension=0,
        tiled=True,
    ).astype(jnp.float32)
    updated = tile_data + layer_scale * (summed.reshape(tile_data.shape) + down_bias)
    pooled = jnp.mean(updated, axis=1)
    embedded = layer_norm(pooled, head_gain, head_bias, 1e-06).astype(jnp.bfloat16)
    seq_rows = jnp.concatenate([embedded, embed_store[0, fresh_count:]], axis=0)
    projected = jnp.dot(
        seq_rows,
        lax.all_gather(in_weight, "slide", axis=0, tiled=True),
        preferred_element_type=jnp.float32,
    )
    normed_seq = layer_norm(projected, slide_gain, 0.0, 1e-05).astype(jnp.bfloat16)
    full_weight = lax.all_gather(qkv_weight, "slide", axis=1, tiled=True)
    packed = normalize_heads(jnp.dot(normed_seq, full_weight, preferred_element_type=jnp.float32))
    local_heads = lax.all_to_all(packed, "slide", split_axis=1, concat_axis=0, tiled=True)
    seq_len = local_heads.shape[0]
    heads_here = local_heads.shape[1] // (3 * HDIM)
    arranged = local_heads.reshape(seq_len, heads_here, 3, HDIM)
    queries = arranged[:, :, 0]
    key_rows = arranged[:, :, 1]
    value_rows = arranged[:, :, 2]
    my_slopes = lax.dynamic_slice_in_dim(
        head_slopes, lax.axis_index("slide") * heads_here, heads_here, 0
    )
    coord_x = tile_coords[0, 0].astype(jnp.float32)
    coord_y = tile_coords[0, 1].astype(jnp.float32)
    valid = valid_counts[0]
    key_ok = jnp.arange(seq_len, dtype=jnp.int32) < valid
    inv_root = 1.0 / math.sqrt(HDIM)
    block_len = min(512, seq_len)
    block_count = seq_len // block_len

    def one_block(block_index):
        first_row = block_index * block_len
        query_block = lax.dynamic_slice_in_dim(queries, first_row, block_len, 0)
        query_x = lax.dynamic_slice_in_dim(coord_x, first_row, block_len, 0)
        query_y = lax.dynamic_slice_in_dim(coord_y, first_row, block_len, 0)
        distance = jnp.abs(query_x[:, None] - coord_x[None, :]) + jnp.abs(
            query_y[:, None] - coord_y[None, :]
        )
        scores = (
            jnp.einsum("qhd,khd->hqk", query_block, key_rows, preferred_element_type=jnp.float32)
            * inv_root
            - my_slopes[:, None, None] * distance[None]
        )
        weights = jnp.where(key_ok[None, None, :], jnp.exp(scores), 0.0).astype(jnp.bfloat16)
        totals = jnp.sum(weights, axis=-1, dtype=jnp.float32)
        weighted = jnp.einsum(
            "hqk,khd->qhd", weights, value_rows, preferred_element_type=jnp.float32
        )
        query_ok = first_row + jnp.arange(block_len, dtype=jnp.int32) < valid
        safe = jnp.where(query_ok[None, :], totals, 1.0)
        result = jnp.where(query_ok[:, None, None], weighted / safe.T[:, :, None], 0.0)
        return result.astype(jnp.bfloat16).reshape(block_len, heads_here * HDIM)

    attended = lax.map(one_block, jnp.arange(block_count, dtype=jnp.int32)).reshape(
        seq_len, heads_here * HDIM
    )
    context = lax.all_to_all(attended, "slide", split_axis=0, concat_axis=1, tiled=True)
    return (embedded[None], context[None])


def solution(mesh):
    in_specs = (
        P(("groups", "rep", "section"), "slide", None, None),
        P(),
        P(),
        P(),
        P(),
        P(None, "rep"),
        P("rep"),
        P("rep", None),
        P(),
        P(),
        P(),
        P(),
        P(("groups", "rep", "section"), "slide", None),
        P("slide", None),
        P(),
        P(None, "slide"),
        P(),
        P(("groups", "rep", "section"), None, None),
        P(("groups", "rep", "section")),
    )
    out_specs = (
        P(("groups", "rep", "section"), "slide", None),
        P(("groups", "rep", "section"), "slide", None),
    )
    return jax.shard_map(
        on_device, mesh=mesh, in_specs=in_specs, out_specs=out_specs, check_vma=False
    )
```

profile of v0, /device:TPU:0, one launch (start us, length us, event | category | flops | bytes accessed | tf_op | source)
XLA Modules:
  0.0 245.6 jit_solution(2592706791371269726)
XLA Ops:
  7.2 0.0 all-gather.4.cloned.1.call-start
  7.2 0.7 all-gather.4.cloned.1.call-update
  7.9 0.0 all-gather.6.cloned.1.call-start
  8.0 0.7 all-gather.6.cloned.1.call-update
  8.7 0.1 reshape.371
  8.8 0.2 slice_reduce_fusion.46
  9.0 0.3 slice_reduce_fusion.47
  9.3 0.3 slice_reduce_fusion.48
  9.7 7.9 %fusion.187 = (f32[3,7,7]{2,1,0:T(8,128)S(1)}, f32[3,7,7,1536]{3,2,1,0:T(8,128)S(1)}) fusion(f32[1536]{0:T(1024)S(1)} %get-tuple-element.81, f32[1536]{0:T(1024)S(1)} %get-tuple-element.82, f32[1536]{0:T(1024)S(1)} %get-tuple-element.25, f32[1536]{0:T(1024)S(1)} %get-tuple-element.26, f32[1536]{0:T(1024)S(1)} %get-tuple-element.27, ...), kind=kLoop, calls=%fused_computation.327 | loop fusion | flops 22353260 | bytes 2114124 | tf_op jit(solution)/shard_map/reduce_sum | solution.py:13
  17.6 0.1 reshape.365
  17.7 0.1 div.47
  17.8 0.3 multiply_reduce_fusion.1
  18.1 0.1 rsqrt.36
  18.2 0.1 copy-done.6
  18.3 0.0 copy-done.7
  18.3 0.2 fusion.143
  18.5 0.0 copy-start.13
  18.5 14.3 %all-gather = bf16[2,147,1536]{2,1,0:T(8,128)(2,1)S(1)} all-gather(bf16[1,147,1536]{2,1,0:T(8,128)(2,1)S(1)} %fusion.143), channel_id=1, replica_groups=mesh['groups'=2,'slide'=4,'rep'=2,'section'=2] {'rep'}, dimensions={0}, use_global_device_ids=true | all-gather | bytes 1354752 | tf_op jit(solution)/shard_map/all_gather | solution.py:77
  32.8 0.2 reshape.375
  33.0 0.0 copy-start.1
  33.0 10.5 %convolution_convert_fusion = bf16[294,1536]{1,0:T(8,128)(2,1)S(1)} fusion(bf16[1536,1536]{1,0:T(8,128)(2,1)} %param.26, bf16[294,1536]{1,0:T(8,128)(2,1)S(1)} %reshape.375, bf16[1536,1536]{1,0:T(8,128)(2,1)} %param.24, f32[1536]{0:T(1024)S(1)} %copy-done.13), kind=kOutput, calls=%fused_computation.52 | convolution fusion | flops 2804788224 | bytes 11249664 | tf_op jit(solution)/shard_map/dot_general | solution.py:85
  43.6 0.0 copy-start.12
  43.6 14.9 %fusion = bf16[152,1536]{1,0:T(8,128)(2,1)S(1)} fusion(bf16[294,1536]{1,0:T(8,128)(2,1)S(1)} %convolution_convert_fusion), kind=kCustom, calls=%all-reduce-scatter | all-reduce-scatter fusion | flops 466945 | bytes 1370624
  58.6 2.7 %collective-permute-start = (bf16[5,1536]{1,0:T(8,128)(2,1)S(1)}, bf16[5,1536]{1,0:T(8,128)(2,1)S(1)}, u32[]{:S(2)}, u32[]{:S(2)}) collective-permute-start(bf16[5,1536]{1,0:T(8,128)(2,1)S(1)} %slice.427), channel_id=1, source_target_pairs={{0,2},{1,3},{4,6},{5,7},{8,10},{9,11},{12,14},{13,15},{16,18},{17,... | collective-permute-start | bytes 46088
  61.3 0.1 slice_bitcast_fusion
  61.4 0.6 dynamic-slice.4
  62.6 0.6 concatenate.9
  63.2 0.0 copy-start.8
  63.2 0.0 copy-start.9
  63.2 0.1 dynamic-slice_convert_fusion
  63.4 0.0 copy-start.3
  63.4 0.0 copy-start.4
  63.4 0.1 reshape.373
  63.5 0.4 copy-done.8
  63.9 0.0 copy-done.9
  63.9 0.2 fusion.111
  64.1 0.1 multiply_reduce_fusion.4
  64.3 0.2 multiply_reduce_fusion.3
  64.5 0.1 add_convert_fusion.1
  64.6 0.0 copy-start.10
  64.6 11.2 %all-gather.4.cloned.1.call-done = bf16[1536,1024]{1,0:T(8,128)(2,1)} async-done(((bf16[384,1024]{1,0:T(8,128)(2,1)}), bf16[1536,1024]{1,0:T(8,128)(2,1)}) %all-gather.4.cloned.1.call-update) | async-done | bytes 3145744 | tf_op jit(solution)/shard_map/all_gather | solution.py:96
  75.8 2.6 %fusion.189 = (f32[128]{0:T(128)S(1)}, f32[128,1024]{1,0:T(8,128)S(1)}) fusion(bf16[1536,1024]{1,0:T(8,128)(2,1)} %all-gather.4.cloned.1.call-done, bf16[125,1536]{1,0:T(8,128)(2,1)S(1)} %slice_bitcast_fusion, bf16[3,1536]{1,0:T(4,128)(2,1)S(1)} %add_convert_fusion.1), kind=kOutput, calls=%fused_computation.328 | convolution fusion | flops 403570560 | bytes 4063744 | tf_op jit(solution)/shard_map/dot_general | solution.py:94
  78.4 0.2 multiply_reduce_fusion.2
  78.6 112.8 %all-gather.6.cloned.1.call-done = bf16[1024,3072]{1,0:T(8,128)(2,1)} async-done(((bf16[1024,768]{1,0:T(8,128)(2,1)}), bf16[1024,3072]{1,0:T(8,128)(2,1)}) %all-gather.6.cloned.1.call-update) | async-done | bytes 6291472 | tf_op jit(solution)/shard_map/all_gather | solution.py:100
  191.4 5.4 %fusion.148 = f32[128,3072]{0,1:T(8,128)S(1)} fusion(bf16[1024,3072]{1,0:T(8,128)(2,1)} %all-gather.6.cloned.1.call-done, f32[128,1024]{1,0:T(8,128)S(1)} %get-tuple-element.88, f32[1024]{0:T(1024)S(1)} %copy-done.10, f32[128]{0:T(128)S(1)} %add_rsqrt_fusion.2, f32[128]{0:T(128)S(1)} %broadcast_multiply_fusion.1), kind=kOutput, calls=%fused_computation.221 | convolution fusion | flops 805830656 | bytes 8393728 | tf_op jit(solution)/shard_map/dot_general | solution.py:101
  196.9 0.1 multiply_reduce_fusion
  197.1 0.1 multiply_convert_fusion
  197.2 0.0 copy-start.14
  197.2 0.0 copy-start.11
  197.2 1.0 pad_maximum_fusion
  198.2 3.5 %all-to-all-start = ((bf16[128,4,768]{0,2,1:T(8,128)(2,1)}), bf16[128,4,768]{0,2,1:T(8,128)(2,1)S(1)}, u32[]{:S(2)}, u32[]{:S(2)}) async-start(bf16[128,4,768]{0,2,1:T(8,128)(2,1)} %bitcast.6), calls=%async_computation | async-start | bytes 1572864 | tf_op jit(solution)/shard_map/all_to_all | solution.py:102
  202.3 0.1 dynamic_slice.12
  202.4 0.2 abs_add_fusion
  202.7 19.6 %all-to-all-done = bf16[128,4,768]{0,2,1:T(8,128)(2,1)S(1)} async-done(((bf16[128,4,768]{0,2,1:T(8,128)(2,1)}), bf16[128,4,768]{0,2,1:T(8,128)(2,1)S(1)}, u32[]{:S(2)}, u32[]{:S(2)}) %all-to-all-start) | async-done | bytes 786464 | tf_op jit(solution)/shard_map/all_to_all | solution.py:102
  222.2 0.6 copy.31
  222.9 0.3 reshape.369
  223.2 1.5 convert_reduce_fusion
  224.7 0.5 fusion.13
  225.1 0.1 all_to_all.24
  225.2 0.7 copy.36
  225.9 3.4 %all-to-all-start.1 = ((bf16[4,128,256]{1,2,0:T(8,128)(2,1)}), bf16[4,128,256]{1,2,0:T(8,128)(2,1)S(1)}, u32[]{:S(2)}, u32[]{:S(2)}) async-start(bf16[4,128,256]{1,2,0:T(8,128)(2,1)} %copy.36), calls=%async_computation.1 | async-start | bytes 524288 | tf_op jit(solution)/shard_map/all_to_all | solution.py:146
  229.4 0.7 fusion.155
  230.0 7.8 %all-to-all-done.1 = bf16[4,128,256]{1,2,0:T(8,128)(2,1)S(1)} async-done(((bf16[4,128,256]{1,2,0:T(8,128)(2,1)}), bf16[4,128,256]{1,2,0:T(8,128)(2,1)S(1)}, u32[]{:S(2)}, u32[]{:S(2)}) %all-to-all-start.1) | async-done | bytes 262176 | tf_op jit(solution)/shard_map/all_to_all | solution.py:146
  237.9 0.8 copy.37
  (29 shorter events, 0.2 us)
Async XLA Ops:
  7.2 1.5 copy-start
  7.2 1.7 copy-start.2
  7.2 68.7 %all-gather.4.cloned.1.call-start = ((), (), s32[]{:S(2)}) async-start(), calls=%async_computation.2 | async-start | bytes 3932160 | tf_op jit(solution)/shard_map/all_gather | solution.py:96
  7.9 1.8 copy-start.5
  7.9 183.5 %all-gather.6.cloned.1.call-start = ((), (), s32[]{:S(2)}) async-start(), calls=%async_computation.3 | async-start | bytes 7864320 | tf_op jit(solution)/shard_map/all_gather | solution.py:100
  17.5 0.7 copy-start.6
  17.5 0.7 copy-start.7
  18.5 14.5 %copy-start.13 = (f32[1536]{0:T(1024)S(1)}, f32[1536]{0:T(1024)}, u32[]{:S(2)}) copy-start(f32[1536]{0:T(1024)} %param.25) | copy-start | bytes 18436
  33.0 28.2 %copy-start.1 = (bf16[1,128,1536]{2,1,0:T(8,128)(2,1)S(1)}, bf16[1,128,1536]{2,1,0:T(8,128)(2,1)}, u32[]{:S(2)}) copy-start(bf16[1,128,1536]{2,1,0:T(8,128)(2,1)} %param.31) | copy-start | bytes 1179652
  43.6 17.8 %copy-start.12 = (u32[32]{0:T(128)S(1)}, u32[32]{0:T(128)}, u32[]{:S(2)}) copy-start(u32[32]{0:T(128)} %constant.125) | copy-start | bytes 388
  58.6 4.1 %collective-permute-start = (bf16[5,1536]{1,0:T(8,128)(2,1)S(1)}, bf16[5,1536]{1,0:T(8,128)(2,1)S(1)}, u32[]{:S(2)}, u32[]{:S(2)}) collective-permute-start(bf16[5,1536]{1,0:T(8,128)(2,1)S(1)} %slice.427), channel_id=1, source_target_pairs={{0,2},{1,3},{4,6},{5,7},{8,10},{9,11},{12,14},{13,15},{16,18},{17,... | collective-permute-start | bytes 46088
  63.2 0.7 copy-start.8
  63.2 0.7 copy-start.9
  63.4 1.1 copy-start.3
  63.4 1.1 copy-start.4
  64.6 126.9 %copy-start.10 = (f32[1024]{0:T(1024)S(1)}, f32[1024]{0:T(1024)}, u32[]{:S(2)}) copy-start(f32[1024]{0:T(1024)} %param.33) | copy-start | bytes 12292
  197.2 5.1 %copy-start.14 = (f32[16]{0:T(128)S(1)}, f32[16]{0:T(128)}, u32[]{:S(2)}) copy-start(f32[16]{0:T(128)} %param.35) | copy-start | bytes 196
  197.2 5.2 %copy-start.11 = (s32[1,2,512]{2,1,0:T(2,128)S(1)}, s32[1,2,512]{2,1,0:T(2,128)}, u32[]{:S(2)}) copy-start(s32[1,2,512]{2,1,0:T(2,128)} %param.36) | copy-start | bytes 12292
  198.2 24.1 %all-to-all-start = ((bf16[128,4,768]{0,2,1:T(8,128)(2,1)}), bf16[128,4,768]{0,2,1:T(8,128)(2,1)S(1)}, u32[]{:S(2)}, u32[]{:S(2)}) async-start(bf16[128,4,768]{0,2,1:T(8,128)(2,1)} %bitcast.6), calls=%async_computation | async-start | bytes 1572864 | tf_op jit(solution)/shard_map/all_to_all | solution.py:102
  225.9 11.9 %all-to-all-start.1 = ((bf16[4,128,256]{1,2,0:T(8,128)(2,1)}), bf16[4,128,256]{1,2,0:T(8,128)(2,1)S(1)}, u32[]{:S(2)}, u32[]{:S(2)}) async-start(bf16[4,128,256]{1,2,0:T(8,128)(2,1)} %copy.36), calls=%async_computation.1 | async-start | bytes 524288 | tf_op jit(solution)/shard_map/all_to_all | solution.py:146
Sparse Core Ops, SparseCore 0:
  9.6 66.2 all-gather.3
  77.4 113.9 all-gather.5
where the time goes:
time: 246 us
  waiting for transfers between devices  153 us (62%)
  blocking collectives  29.3 us (12%)
  matrix products  20.5 us (8%)
  between operations  15.7 us (6%)
  other arithmetic  11.5 us (5%)
  starting transfers between devices  9.67 us (4%)
  local copies, waits for them, and re-layouts  6.05 us (2%)
    all_gather x1, waiting for transfers between devices, on_device(): full_weight = lax.all_gather(qkv_weight, 'slide', axis=1, tiled=True)  113 us
    all_to_all x1, waiting for transfers between devices, on_device(): lax.all_to_all(packed, 'slide', split_axis=1, concat_axis=0, tiled=True)  19.6 us
    unnamed x1, blocking collectives  14.9 us
    all_gather x1, blocking collectives, on_device(): lax.all_gather(normed, 'rep', axis=0, tiled=True)  14.3 us
    all_gather x1, waiting for transfers between devices, on_device(): lax.all_gather(in_weight, 'slide', axis=0, tiled=True)  11.2 us
    dot_general x1, matrix products, on_device(): jnp.dot(hidden, down_weight, preferred_element_type=jnp.float32)  10.5 us
    reduce_sum x2, other arithmetic, layer_norm(): center = jnp.mean(inputs, axis=-1, keepdims=True)  8 us
    all_to_all x1, waiting for transfers between devices, on_device(): lax.all_to_all(attended, 'slide', split_axis=0, concat_axis=1, tiled=True)  7.82 us
  transfers between devices with their start and end apart: 5, of which 4 were waited for; matrix products, arithmetic and copies ran while one was open for 17% of the time, Pallas kernels for 0%

commit v1 on v0

--- a/solution.py
+++ b/solution.py
@@ -97,7 +97,14 @@
         preferred_element_type=jnp.float32,
     )
     normed_seq = layer_norm(projected, slide_gain, 0.0, 1e-05).astype(jnp.bfloat16)
-    full_weight = lax.all_gather(qkv_weight, "slide", axis=1, tiled=True)
+    count = lax.axis_size("slide")
+    right = [(i, (i + 1) % count) for i in range(count)]
+    terms = [qkv_weight]
+    for far in range(1, count):
+        terms = [lax.ppermute(terms[0], "slide", right), *terms]
+    whole = jnp.concatenate(terms, axis=1)
+    offset = (lax.axis_index("slide") + 1) * terms[-1].shape[1]
+    full_weight = jnp.roll(whole, offset, axis=1)
     packed = normalize_heads(jnp.dot(normed_seq, full_weight, preferred_element_type=jnp.float32))
     local_heads = lax.all_to_all(packed, "slide", split_axis=1, concat_axis=0, tiled=True)
     seq_len = local_heads.shape[0]

time: 246 us -> 226 us (0.919)
  waiting for transfers between devices: 153 us -> 74.1 us
  starting transfers between devices: 9.67 us -> 35.7 us
  other arithmetic: 11.5 us -> 31.5 us
  local copies, waits for them, and re-layouts: 6.05 us -> 20.2 us
  blocking collectives: 29.3 us -> 25.8 us
    all_gather x1 -> x0, waiting for transfers between devices: 113 us -> none  [on_device(): full_weight = lax.all_gather(qkv_weight, 'slide', axis=1, tiled=True)]
    ppermute x0 -> x3, waiting for transfers between devices: none -> 52.1 us  [on_device(): terms = [lax.ppermute(terms[0], 'slide', right), *terms]]
    ppermute x0 -> x3, starting transfers between devices: none -> 26.2 us  [on_device(): terms = [lax.ppermute(terms[0], 'slide', right), *terms]]
    reduce_sum x2, other arithmetic: 8 us -> 24.9 us  [layer_norm(): center = jnp.mean(inputs, axis=-1, keepdims=True)]
    all_gather x1, waiting for transfers between devices: 11.2 us -> 0.02 us  [on_device(): lax.all_gather(in_weight, 'slide', axis=0, tiled=True)]
    unnamed x35 -> x36, local copies, waits for them, and re-layouts: 2.75 us -> 11 us
    all_to_all x1, waiting for transfers between devices: 19.6 us -> 15.2 us  [on_device(): lax.all_to_all(packed, 'slide', split_axis=1, concat_axis=0, tiled=True)]
    slice x3, local copies, waits for them, and re-layouts: 0.82 us -> 4.82 us  [depthwise(): depth_weight[tap_row * KER + tap_col]]
  transfers between devices with their start and end apart: 5 -> 7, of which waited for: 4 -> 5; matrix products, arithmetic and copies ran while one was open for 17% -> 29% of each run, Pallas kernels for 0% -> 0%
where the time goes in v1:
time: 226 us; the launch traced here: 225 us
  waiting for transfers between devices  74.1 us (33%)
  starting transfers between devices  35.7 us (16%)
  other arithmetic  31.5 us (14%)
  blocking collectives  25.8 us (11%)
  matrix products  21.5 us (10%)
  local copies, waits for them, and re-layouts  20.2 us (9%)
  between operations  15.8 us (7%)
    ppermute x3, waiting for transfers between devices, on_device(): terms = [lax.ppermute(terms[0], 'slide', right), *terms]  52.1 us
    ppermute x3, starting transfers between devices, on_device(): terms = [lax.ppermute(terms[0], 'slide', right), *terms]  26.2 us
    reduce_sum x2, other arithmetic, layer_norm(): center = jnp.mean(inputs, axis=-1, keepdims=True)  24.9 us
    all_to_all x1, waiting for transfers between devices, on_device(): lax.all_to_all(packed, 'slide', split_axis=1, concat_axis=0, tiled=True)  15.2 us
    all_gather x1, blocking collectives, on_device(): lax.all_gather(normed, 'rep', axis=0, tiled=True)  13 us
    unnamed x1, blocking collectives  12.8 us
    dot_general x1, matrix products, on_device(): jnp.dot(hidden, down_weight, preferred_element_type=jnp.float32)  11.4 us
    unnamed x36, local copies, waits for them, and re-layouts  11 us
  transfers between devices with their start and end apart: 7, of which 5 were waited for; matrix products, arithmetic and copies ran while one was open for 29% of the time, Pallas kernels for 0%

profile of v1, /device:TPU:0, one launch (start us, length us, event | category | flops | bytes accessed | tf_op | source)
XLA Modules:
  0.0 224.6 jit_solution(17833632522492874080)
XLA Ops:
  7.2 0.0 all-gather.3.cloned.1.call-start
  7.2 0.7 all-gather.3.cloned.1.call-update
  7.9 3.1 %collective-permute-start = (bf16[1024,768]{1,0:T(8,128)(2,1)}, bf16[1024,768]{1,0:T(8,128)(2,1)S(1)}, u32[]{:S(2)}, u32[]{:S(2)}) collective-permute-start(bf16[1024,768]{1,0:T(8,128)(2,1)} %param.34), channel_id=1, source_target_pairs={{0,4},{4,8},{8,12},{12,0},{1,5},{5,9},{9,13},{13,1},{2,6},{6,10},{... | collective-permute-start | bytes 4718600 | tf_op jit(solution)/shard_map/ppermute | solution.py:104
  11.0 1.8 slice_reduce_fusion.48
  12.8 1.7 slice_reduce_fusion.47
  14.6 1.3 slice_reduce_fusion.46
  15.8 1.1 reshape.371
  16.9 24.7 %fusion.189 = (f32[3,7,7]{2,1,0:T(8,128)S(1)}, f32[3,7,7,1536]{3,2,1,0:T(8,128)S(1)}) fusion(f32[1536]{0:T(1024)S(1)} %get-tuple-element.81, f32[1536]{0:T(1024)S(1)} %get-tuple-element.82, f32[1536]{0:T(1024)S(1)} %get-tuple-element.25, f32[1536]{0:T(1024)S(1)} %get-tuple-element.26, f32[1536]{0:T(1024)S(1)} %get-tuple-element.27, ...), kind=kLoop, calls=%fused_computation.337 | loop fusion | flops 22353260 | bytes 2114124 | tf_op jit(solution)/shard_map/reduce_sum | solution.py:13
  41.7 0.1 reshape.365
  41.8 0.9 multiply_reduce_fusion.1
  42.7 0.1 div.47
  42.8 0.7 add_rsqrt_fusion.1
  43.5 0.1 rsqrt.36
  43.6 0.9 fusion.145
  44.6 13.0 %all-gather = bf16[2,147,1536]{2,1,0:T(8,128)(2,1)S(1)} all-gather(bf16[1,147,1536]{2,1,0:T(8,128)(2,1)S(1)} %fusion.145), channel_id=1, replica_groups=mesh['groups'=2,'slide'=4,'rep'=2,'section'=2] {'rep'}, dimensions={0}, use_global_device_ids=true | all-gather | bytes 1354752 | tf_op jit(solution)/shard_map/all_gather | solution.py:77
  57.6 0.2 reshape.375
  57.8 0.0 copy-start.3
  57.8 11.4 %convolution_convert_fusion = bf16[294,1536]{1,0:T(8,128)(2,1)} fusion(bf16[1536,1536]{1,0:T(8,128)(2,1)} %param.26, bf16[294,1536]{1,0:T(8,128)(2,1)S(1)} %reshape.375, bf16[1536,1536]{1,0:T(8,128)(2,1)} %param.24, f32[1536]{0:T(1024)S(1)} %copy-done.10), kind=kOutput, calls=%fused_computation.54 | convolution fusion | flops 2804788224 | bytes 11249664 | tf_op jit(solution)/shard_map/dot_general | solution.py:85
  69.3 2.0 collective-permute-done
  71.2 23.1 %collective-permute-start.1 = (bf16[1024,768]{1,0:T(8,128)(2,1)S(1)}, bf16[1024,768]{1,0:T(8,128)(2,1)}, u32[]{:S(2)}, u32[]{:S(2)}) collective-permute-start(bf16[1024,768]{1,0:T(8,128)(2,1)S(1)} %collective-permute-done), channel_id=1, source_target_pairs={{0,4},{4,8},{8,12},{12,0},{1,5},{5,9},{9,13},{13,1},{2,6},{6,10},{... | collective-permute-start | bytes 4718600 | tf_op jit(solution)/shard_map/ppermute | solution.py:104
  94.3 12.8 %fusion = bf16[152,1536]{1,0:T(8,128)(2,1)S(1)} fusion(bf16[294,1536]{1,0:T(8,128)(2,1)} %convolution_convert_fusion), kind=kCustom, calls=%all-reduce-scatter | all-reduce-scatter fusion | flops 466945 | bytes 1370624
  107.1 2.6 %collective-permute-start.3 = (bf16[5,1536]{1,0:T(8,128)(2,1)S(1)}, bf16[5,1536]{1,0:T(8,128)(2,1)S(1)}, u32[]{:S(2)}, u32[]{:S(2)}) collective-permute-start(bf16[5,1536]{1,0:T(8,128)(2,1)S(1)} %slice.427), channel_id=1, source_target_pairs={{0,2},{1,3},{4,6},{5,7},{8,10},{9,11},{12,14},{13,15},{16,18},{17,... | collective-permute-start | bytes 46088
  109.7 0.9 slice_bitcast_fusion
  110.6 0.6 dynamic-slice.4
  111.9 0.6 concatenate.16
  112.4 0.1 dynamic-slice_convert_fusion
  112.6 0.1 reshape.373
  112.7 1.3 fusion.113
  114.0 0.1 multiply_reduce_fusion.4
  114.2 0.2 multiply_reduce_fusion.3
  114.4 18.0 %collective-permute-done.1 = bf16[1024,768]{1,0:T(8,128)(2,1)} collective-permute-done((bf16[1024,768]{1,0:T(8,128)(2,1)S(1)}, bf16[1024,768]{1,0:T(8,128)(2,1)}, u32[]{:S(2)}, u32[]{:S(2)}) %collective-permute-start.1) | collective-permute-done | bytes 1572896 | tf_op jit(solution)/shard_map/ppermute | solution.py:104
  132.4 0.1 add_convert_fusion.1
  132.5 0.0 all-gather.3.cloned.1.call-done
  132.5 2.5 %fusion.191 = (f32[128]{0:T(128)S(1)}, f32[128,1024]{1,0:T(8,128)S(1)}) fusion(bf16[1536,1024]{1,0:T(8,128)(2,1)} %all-gather.3.cloned.1.call-done, bf16[125,1536]{1,0:T(8,128)(2,1)S(1)} %copy-done.2, bf16[3,1536]{1,0:T(4,128)(2,1)S(1)} %add_convert_fusion.1), kind=kOutput, calls=%fused_computation.338 | convolution fusion | flops 403570560 | bytes 4063744 | tf_op jit(solution)/shard_map/dot_general | solution.py:94
  135.1 0.2 multiply_reduce_fusion.2
  135.3 32.1 %collective-permute-done.2 = bf16[1024,768]{1,0:T(8,128)(2,1)} collective-permute-done((bf16[1024,768]{1,0:T(8,128)(2,1)}, bf16[1024,768]{1,0:T(8,128)(2,1)}, u32[]{:S(2)}, u32[]{:S(2)}) %collective-permute-start.2) | collective-permute-done | bytes 1572896 | tf_op jit(solution)/shard_map/ppermute | solution.py:104
  167.4 1.6 constant_dynamic-update-slice_fusion.7
  169.0 1.6 constant_dynamic-update-slice_fusion.6
  170.7 0.2 constant_dynamic-update-slice_fusion.5
  170.9 1.2 copy-done
  172.1 0.2 constant_dynamic-update-slice_fusion.4
  172.3 1.6 constant_dynamic-update-slice_fusion.3
  173.9 1.6 constant_dynamic-update-slice_fusion.2
  175.5 0.2 constant_dynamic-update-slice_fusion.1
  175.8 0.2 constant_dynamic-update-slice_fusion
  176.0 0.5 copy-done.7
  176.5 5.6 %fusion.1 = f32[128,3072]{0,1:T(8,128)S(1)} fusion(bf16[1024,6144]{1,0:T(8,128)(2,1)S(1)} %constant_dynamic-update-slice_fusion, s32[]{:T(128)S(6)} %select_n.40, f32[128,1024]{1,0:T(8,128)S(1)} %get-tuple-element.88, f32[1024]{0:T(1024)S(1)} %copy-done.7, f32[128]{0:T(128)S(1)} %add_rsqrt_fusion.2, f32[128]{0:T(128)S(1)} %broadcast_multiply_fusion.1), kind=kOutput, calls=%fused_computation.48 | convolution fusion | flops 805830656 | bytes 8393732 | tf_op jit(solution)/shard_map/dot_general | solution.py:108
  182.0 0.1 multiply_reduce_fusion
  182.2 0.1 multiply_convert_fusion
  182.4 1.0 pad_maximum_fusion
  183.3 3.5 %all-to-all-start = ((bf16[128,4,768]{0,2,1:T(8,128)(2,1)}), bf16[128,4,768]{0,2,1:T(8,128)(2,1)S(1)}, u32[]{:S(2)}, u32[]{:S(2)}) async-start(bf16[128,4,768]{0,2,1:T(8,128)(2,1)} %bitcast.6), calls=%async_computation | async-start | bytes 1572864 | tf_op jit(solution)/shard_map/all_to_all | solution.py:109
  187.5 0.1 dynamic_slice.17
  187.6 0.2 abs_add_fusion
  187.8 15.2 %all-to-all-done = bf16[128,4,768]{0,2,1:T(8,128)(2,1)S(1)} async-done(((bf16[128,4,768]{0,2,1:T(8,128)(2,1)}), bf16[128,4,768]{0,2,1:T(8,128)(2,1)S(1)}, u32[]{:S(2)}, u32[]{:S(2)}) %all-to-all-start) | async-done | bytes 786464 | tf_op jit(solution)/shard_map/all_to_all | solution.py:109
  203.1 0.6 copy.31
  203.7 0.3 reshape.369
  204.0 1.5 convert_reduce_fusion
  205.5 0.5 fusion.15
  205.9 0.1 all_to_all.24
  206.0 0.7 copy.36
  206.8 3.4 %all-to-all-start.1 = ((bf16[4,128,256]{1,2,0:T(8,128)(2,1)}), bf16[4,128,256]{1,2,0:T(8,128)(2,1)S(1)}, u32[]{:S(2)}, u32[]{:S(2)}) async-start(bf16[4,128,256]{1,2,0:T(8,128)(2,1)} %copy.36), calls=%async_computation.1 | async-start | bytes 524288 | tf_op jit(solution)/shard_map/all_to_all | solution.py:153
  210.2 0.7 fusion.156
  210.8 6.1 %all-to-all-done.1 = bf16[4,128,256]{1,2,0:T(8,128)(2,1)S(1)} async-done(((bf16[4,128,256]{1,2,0:T(8,128)(2,1)}), bf16[4,128,256]{1,2,0:T(8,128)(2,1)S(1)}, u32[]{:S(2)}, u32[]{:S(2)}) %all-to-all-start.1) | async-done | bytes 262176 | tf_op jit(solution)/shard_map/all_to_all | solution.py:153
  216.9 0.8 copy.37
  (34 shorter events, 0.2 us)
Async XLA Ops:
  7.2 8.7 %copy-start.1 = (bf16[1,3,49,1536]{3,2,1,0:T(8,128)(2,1)S(1)}, bf16[1,3,49,1536]{3,2,1,0:T(8,128)(2,1)}, u32[]{:S(2)}) copy-start(bf16[1,3,49,1536]{3,2,1,0:T(8,128)(2,1)} %param.19) | copy-start | bytes 1354756
  7.2 9.8 %copy-start.6 = (f32[1536]{0:T(1024)S(1)}, f32[1536]{0:T(1024)}, u32[]{:S(2)}) copy-start(f32[1536]{0:T(1024)} %param.21) | copy-start | bytes 18436
  7.2 125.3 %all-gather.3.cloned.1.call-start = ((), (), s32[]{:S(2)}) async-start(), calls=%async_computation.2 | async-start | bytes 3932160 | tf_op jit(solution)/shard_map/all_gather | solution.py:96
  7.9 63.3 %collective-permute-start = (bf16[1024,768]{1,0:T(8,128)(2,1)}, bf16[1024,768]{1,0:T(8,128)(2,1)S(1)}, u32[]{:S(2)}, u32[]{:S(2)}) collective-permute-start(bf16[1024,768]{1,0:T(8,128)(2,1)} %param.34), channel_id=1, source_target_pairs={{0,4},{4,8},{8,12},{12,0},{1,5},{5,9},{9,13},{13,1},{2,6},{6,10},{... | collective-permute-start | bytes 4718600 | tf_op jit(solution)/shard_map/ppermute | solution.py:104
  44.6 13.2 %copy-start.10 = (f32[1536]{0:T(1024)S(1)}, f32[1536]{0:T(1024)}, u32[]{:S(2)}) copy-start(f32[1536]{0:T(1024)} %param.25) | copy-start | bytes 18436
  57.8 51.9 %copy-start.3 = (bf16[1,128,1536]{2,1,0:T(8,128)(2,1)S(1)}, bf16[1,128,1536]{2,1,0:T(8,128)(2,1)}, u32[]{:S(2)}) copy-start(bf16[1,128,1536]{2,1,0:T(8,128)(2,1)} %param.31) | copy-start | bytes 1179652
  69.3 41.4 %copy-start.9 = (u32[32]{0:T(128)S(1)}, u32[32]{0:T(128)}, u32[]{:S(2)}) copy-start(u32[32]{0:T(128)} %constant.147) | copy-start | bytes 388
  71.2 61.1 %collective-permute-start.1 = (bf16[1024,768]{1,0:T(8,128)(2,1)S(1)}, bf16[1024,768]{1,0:T(8,128)(2,1)}, u32[]{:S(2)}, u32[]{:S(2)}) collective-permute-start(bf16[1024,768]{1,0:T(8,128)(2,1)S(1)} %collective-permute-done), channel_id=1, source_target_pairs={{0,4},{4,8},{8,12},{12,0},{1,5},{5,9},{9,13},{13,1},{2,6},{6,10},{... | collective-permute-start | bytes 4718600 | tf_op jit(solution)/shard_map/ppermute | solution.py:104
  107.1 4.7 %collective-permute-start.3 = (bf16[5,1536]{1,0:T(8,128)(2,1)S(1)}, bf16[5,1536]{1,0:T(8,128)(2,1)S(1)}, u32[]{:S(2)}, u32[]{:S(2)}) collective-permute-start(bf16[5,1536]{1,0:T(8,128)(2,1)S(1)} %slice.427), channel_id=1, source_target_pairs={{0,2},{1,3},{4,6},{5,7},{8,10},{9,11},{12,14},{13,15},{16,18},{17,... | collective-permute-start | bytes 46088
  112.6 19.8 %copy-start.4 = (f32[1536]{0:T(1024)S(1)}, f32[1536]{0:T(1024)}, u32[]{:S(2)}) copy-start(f32[1536]{0:T(1024)} %param.30) | copy-start | bytes 18436
  112.6 19.8 %copy-start.5 = (f32[1536]{0:T(1024)S(1)}, f32[1536]{0:T(1024)}, u32[]{:S(2)}) copy-start(f32[1536]{0:T(1024)} %param.29) | copy-start | bytes 18436
  112.7 19.8 %copy-start.2 = (bf16[125,1536]{1,0:T(8,128)(2,1)S(1)}, bf16[125,1536]{1,0:T(8,128)(2,1)}, u32[]{:S(2)}) copy-start(bf16[125,1536]{1,0:T(8,128)(2,1)} %slice_bitcast_fusion) | copy-start | bytes 1152004
  132.3 35.1 %collective-permute-start.2 = (bf16[1024,768]{1,0:T(8,128)(2,1)}, bf16[1024,768]{1,0:T(8,128)(2,1)}, u32[]{:S(2)}, u32[]{:S(2)}) collective-permute-start(bf16[1024,768]{1,0:T(8,128)(2,1)} %collective-permute-done.1), channel_id=1, source_target_pairs={{0,4},{4,8},{8,12},{12,0},{1,5},{5,9},{9,13},{13,1},{2,6},{6,10},{... | collective-permute-start | bytes 4718600 | tf_op jit(solution)/shard_map/ppermute | solution.py:104
  170.7 1.4 copy-start
  175.8 0.7 copy-start.7
  182.3 5.1 %copy-start.11 = (f32[16]{0:T(128)S(1)}, f32[16]{0:T(128)}, u32[]{:S(2)}) copy-start(f32[16]{0:T(128)} %param.35) | copy-start | bytes 196
  182.4 5.2 %copy-start.8 = (s32[1,2,512]{2,1,0:T(2,128)S(1)}, s32[1,2,512]{2,1,0:T(2,128)}, u32[]{:S(2)}) copy-start(s32[1,2,512]{2,1,0:T(2,128)} %param.36) | copy-start | bytes 12292
  183.3 19.7 %all-to-all-start = ((bf16[128,4,768]{0,2,1:T(8,128)(2,1)}), bf16[128,4,768]{0,2,1:T(8,128)(2,1)S(1)}, u32[]{:S(2)}, u32[]{:S(2)}) async-start(bf16[128,4,768]{0,2,1:T(8,128)(2,1)} %bitcast.6), calls=%async_computation | async-start | bytes 1572864 | tf_op jit(solution)/shard_map/all_to_all | solution.py:109
  206.8 10.2 %all-to-all-start.1 = ((bf16[4,128,256]{1,2,0:T(8,128)(2,1)}), bf16[4,128,256]{1,2,0:T(8,128)(2,1)S(1)}, u32[]{:S(2)}, u32[]{:S(2)}) async-start(bf16[4,128,256]{1,2,0:T(8,128)(2,1)} %copy.36), calls=%async_computation.1 | async-start | bytes 524288 | tf_op jit(solution)/shard_map/all_to_all | solution.py:153
Sparse Core Ops, SparseCore 0:
  9.6 91.2 all-gather.2
